TPU v7x, 256 devices: a whole 4x4x8 slice. The times are simulated.
256 devices in a mesh: kv: 8 (over x, core), seq: 32 (over z, y).
Axes of the slice: x: 4, y: 4, z: 8, core: 2. Of those that a mesh axis runs over, the one named last changes fastest.
Arguments:
- hidden_states: bfloat16 [6144, 2048], P('seq')
- attn_gain: float32 [2048], replicated, may hold values from 0.5 to 1.5
- w_q: bfloat16 [2048, 2048], P(None, 'kv')
- w_k: bfloat16 [2048, 512], P(None, 'kv')
- w_v: bfloat16 [2048, 512], P(None, 'kv'), may hold values from -0.125 to 0.125
- w_o: bfloat16 [2048, 2048], P('kv'), may hold values from -0.125 to 0.125
- final_gain: float32 [2048], replicated, may hold values from 0.5 to 1.5
- w_head: bfloat16 [2048, 49408], P(None, ('kv', 'seq'))
- doc_lengths: int32 [26], replicated, may hold values from 1 to 3072, as said below
- target_ids: int32 [6144], replicated, may hold values from 0 to 49154, as said below
- vocab_mask: int32 [49408], P(('kv', 'seq')), may hold values from 0 to 1, as said below
Outputs:
- log_probs: float32 [6144], P('seq')
- entropies: float32 [6144], P('seq')
Inputs may be any that keep to these rules, and one draw needn't show every extreme that they name: `doc_lengths`: they sum to 6144; one is 3072, one more is over 1536, every other is under 64. `target_ids`: each names an entry whose vocab_mask is 1. `vocab_mask`: entries from 49155 on are 0.
All inputs are finite; a program needn't handle non-finite values.
Results may differ from a plain program's by a relative error of at most 0.0045.
Values may be sent and summed in bfloat16 or wider, within the bound.
No kernel may reach another device: no remote copies, remote signals or barrier semaphores. Data moves between devices by JAX's collectives and lax.ppermute only.
A program may use at most 128 MiB of HBM per device.

v0:
```python
import math
import jax
import jax.numpy as jnp
from jax import lax
from jax.sharding import PartitionSpec as P

HEAD_DIM = 64
ROPE_THETA = 10000000.0
NORM_EPS = 1e-05
NEG_FILL = -1e30
ATTN_SCALE = 0.015625
RESID_SCALE = 5.0
LOGIT_SCALE = 0.125


def rms_norm(values, gain_vec):
    return (
        values * lax.rsqrt(jnp.mean(values * values, axis=-1, keepdims=True) + NORM_EPS) * gain_vec
    )


def rotate(values, positions):
    half_dim = values.shape[-1] // 2
    inverse = jnp.exp(
        jnp.arange(half_dim, dtype=jnp.float32) * (-2.0 * math.log(ROPE_THETA) / values.shape[-1])
    )
    angles = positions.astype(jnp.float32)[:, None] * inverse[None, :]
    cos_val = jnp.cos(angles)[:, None, :]
    sine_val = jnp.sin(angles)[:, None, :]
    lower_half = values[..., :half_dim]
    upper_half = values[..., half_dim:]
    return jnp.concatenate(
        [
            lower_half * cos_val - upper_half * sine_val,
            upper_half * cos_val + lower_half * sine_val,
        ],
        axis=-1,
    )


def local(
    hidden_states,
    attn_gain,
    w_q,
    w_k,
    w_v,
    w_o,
    final_gain,
    w_head,
    doc_lengths,
    target_ids,
    vocab_mask,
):
    tok_rows = hidden_states.shape[0]
    seq_index = lax.axis_index("seq")
    kv_local = w_k.shape[1] // HEAD_DIM
    q_local = w_q.shape[1] // HEAD_DIM
    group_size = q_local // kv_local
    key_width = kv_local * HEAD_DIM
    stream = hidden_states.astype(jnp.float32)
    normed_in = rms_norm(stream, attn_gain).astype(jnp.bfloat16)
    queries = jnp.dot(normed_in, w_q, preferred_element_type=jnp.float32)
    key_proj = jnp.dot(normed_in, w_k, preferred_element_type=jnp.float32)
    value_proj = jnp.dot(normed_in, w_v, preferred_element_type=jnp.float32)
    token_pos = seq_index * tok_rows + jnp.arange(tok_rows, dtype=jnp.int32)
    doc_ends = jnp.cumsum(doc_lengths)
    doc_starts = doc_ends - doc_lengths
    doc_start = jnp.max(
        jnp.where(doc_starts[None, :] <= token_pos[:, None], doc_starts[None, :], 0), axis=1
    )
    positions = token_pos - doc_start
    rotated_q = rotate(queries.reshape(tok_rows, q_local, HEAD_DIM), positions).astype(jnp.bfloat16)
    rotated_q = rotated_q.reshape(tok_rows, kv_local, group_size, HEAD_DIM)
    rotated_k = rotate(key_proj.reshape(tok_rows, kv_local, HEAD_DIM), positions).astype(
        jnp.bfloat16
    )
    packed = jnp.concatenate(
        [rotated_k.reshape(tok_rows, key_width), value_proj.astype(jnp.bfloat16)], axis=1
    )
    earliest = doc_start[0]
    latest = token_pos[tok_rows - 1]
    initial = (
        jnp.full((kv_local, group_size, tok_rows), NEG_FILL, jnp.float32),
        jnp.zeros((kv_local, group_size, tok_rows), jnp.float32),
        jnp.zeros((kv_local, group_size, tok_rows, HEAD_DIM), jnp.float32),
    )
    shard_rows = lax.all_gather(packed, "seq", axis=0, tiled=True)
    offset = jnp.int32(0)
    row_count = shard_rows.shape[0]
    key_pos = jnp.arange(row_count, dtype=jnp.int32)

    def update(current):
        top_score, totals, context_sum = current
        key_rows = shard_rows[:, :key_width].reshape(row_count, kv_local, HEAD_DIM)
        value_rows = shard_rows[:, key_width:].reshape(row_count, kv_local, HEAD_DIM)
        scores = (
            jnp.einsum("tkgd,skd->kgts", rotated_q, key_rows, preferred_element_type=jnp.float32)
            * ATTN_SCALE
        )
        allowed = (key_pos[None, :] >= doc_start[:, None]) & (
            key_pos[None, :] <= token_pos[:, None]
        )
        scores = jnp.where(allowed, scores, NEG_FILL)
        new_top = jnp.maximum(top_score, jnp.max(scores, axis=-1))
        weights = jnp.where(allowed, jnp.exp(scores - new_top[..., None]), 0.0)
        rescale = jnp.exp(top_score - new_top)
        totals = jnp.sum(weights, axis=-1)
        context_sum = jnp.einsum(
            "kgts,skd->kgtd",
            weights.astype(jnp.bfloat16),
            value_rows,
            preferred_element_type=jnp.float32,
        )
        return (new_top, totals, context_sum)

    skip_piece = (offset + row_count <= earliest) | (offset > latest)
    top_score, totals, context_sum = lax.cond(skip_piece, lambda current: current, update, initial)
    context = (
        (context_sum / totals[..., None])
        .transpose(2, 0, 1, 3)
        .reshape(tok_rows, q_local * HEAD_DIM)
        .astype(jnp.bfloat16)
    )
    vocab_local = w_head.shape[1]
    flat_rank = lax.axis_index(("kv", "seq"))
    live_mask = vocab_mask == 1
    columns = flat_rank * vocab_local + jnp.arange(vocab_local, dtype=jnp.int32)
    attn_out = lax.psum(jnp.dot(context, w_o, preferred_element_type=jnp.float32), "kv")
    final_in = rms_norm(stream + RESID_SCALE * attn_out, final_gain).astype(jnp.bfloat16)
    head_shard_rows = lax.all_gather(final_in, "seq", axis=0, tiled=True)
    logits = jnp.dot(head_shard_rows, w_head, preferred_element_type=jnp.float32) * LOGIT_SCALE
    masked = jnp.where(live_mask[None, :], logits, NEG_FILL)
    top_row = jnp.max(masked, axis=1)
    shifted = jnp.where(live_mask[None, :], masked - top_row[:, None], 0.0)
    expw = jnp.where(live_mask[None, :], jnp.exp(shifted), 0.0)
    target = jnp.sum(jnp.where(target_ids[:, None] == columns[None, :], logits, 0.0), axis=1)
    row_stats = jnp.stack([top_row, jnp.sum(expw, axis=1), jnp.sum(expw * shifted, axis=1), target])
    top_all = lax.pmax(row_stats[0], ("kv", "seq"))
    rescale = jnp.exp(row_stats[0] - top_all)
    total_all, spread_all, target_all = lax.psum(
        (
            row_stats[1] * rescale,
            rescale * (row_stats[2] + (row_stats[0] - top_all) * row_stats[1]),
            row_stats[3],
        ),
        ("kv", "seq"),
    )
    log_prob = target_all - top_all - jnp.log(total_all)
    entropy = jnp.log(total_all) - spread_all / total_all
    log_probs = lax.dynamic_slice_in_dim(log_prob, seq_index * tok_rows, tok_rows, 0)
    entropies = lax.dynamic_slice_in_dim(entropy, seq_index * tok_rows, tok_rows, 0)
    return (log_probs, entropies)


def solution(mesh):
    in_specs = (
        P("seq", None),
        P(),
        P(None, "kv"),
        P(None, "kv"),
        P(None, "kv"),
        P("kv", None),
        P(),
        P(None, ("kv", "seq")),
        P(),
        P(),
        P(("kv", "seq")),
    )
    out_specs = (P("seq"), P("seq"))
    return jax.shard_map(local, mesh=mesh, in_specs=in_specs, out_specs=out_specs, check_vma=False)
```

profile of v0, /device:TPU:1, one launch (start us, length us, event | category | flops | bytes accessed | tf_op | source)
XLA Modules:
  0.0 718.2 jit_solution(9096987467154612652)
XLA Ops:
  7.2 0.0 copy-start
  7.2 0.0 copy-start.1
  7.2 0.0 copy-start.6
  7.2 0.0 all-gather.3.cloned.1.call-start
  7.3 1.5 fusion.16
  8.8 0.8 copy.22
  9.6 0.1 reduce.2
  9.7 0.7 sub.45
  10.4 0.1 select_reduce_fusion.2
  10.5 1.6 convolution_convert_fusion
  12.2 1.6 convolution_bitcast_fusion
  13.8 0.2 fusion.30
  14.0 0.7 copy.23
  14.7 0.0 all-gather.3.cloned.1.call-update
  14.8 0.0 all-reduce.4.cloned.1.call-start
  14.8 0.6 slice.25
  15.4 0.5 slice.24
  17.2 0.2 multiply_cosine_fusion
  17.4 0.0 copy-done.1
  17.5 0.6 fusion.33
  18.2 73.0 %all-gather.3.cloned.1.call-done = bf16[6144,128]{1,0:T(8,128)(2,1)} async-done(((bf16[192,128]{1,0:T(8,128)(2,1)}), bf16[6144,128]{1,0:T(8,128)(2,1)}) %all-gather.3.cloned.1.call-update) | async-done | bytes 1572880 | tf_op jit(solution)/shard_map/all_gather | solution.py:87
  91.2 21.4 %conditional.1 = (f32[1,4,192]{2,1,0:T(4,128)S(1)}, f32[1,4,192,64]{2,3,1,0:T(8,128)S(1)}) conditional(s32[]{:T(128)} %bitcast.9, (s32[6144]{0:T(1024)S(1)}, s32[6144]{0:T(1024)S(1)}, s32[192]{0:T(256)S(1)}, s32[192]{0:T(256)S(1)}, bf16[6144,128]{1,0:T(8,128)(2,1)}, /*index=5*/bf16[192,1,4,64]{0,3,2,1:T(8,128)(2,1)S(1)}) %tuple.16, () %tuple.17), branch_computations={%region_3.6_spmd, %region_6.7_spmd} | conditional | flops 1272839424 | bytes 66424336 | solution.py:117
  91.2 1.0 compare_and_fusion
  92.2 2.6 copy.25
  94.8 5.0 fusion
  99.8 6.3 fusion.7
  106.1 6.5 fusion.2
  112.6 0.0 copy-start.3
  112.6 0.0 copy-start.7
  112.6 0.0 copy-start.5
  112.6 1.6 fusion.37
  114.2 0.0 all-reduce.4.cloned.1.call-update
  114.2 0.2 all-gather.5.cloned.1.call-start
  114.5 69.0 %all-reduce.4.cloned.1.call-done = f32[192,2048]{1,0:T(8,128)} async-done(((f32[192,2048]{1,0:T(8,128)}), f32[192,2048]{1,0:T(8,128)}) %all-reduce.4.cloned.1.call-update) | async-done | bytes 1572880 | tf_op jit(solution)/shard_map/psum | solution.py:128
  183.5 1.7 multiply_reduce_fusion.1
  185.2 2.6 multiply_convert_fusion
  187.9 0.0 all-gather.5.cloned.1.call-update
  187.9 0.0 all-reduce.6.cloned.1.call-start
  188.0 0.0 copy-start.2
  188.0 184.3 %all-gather.5.cloned.1.call-done = bf16[6144,2048]{1,0:T(8,128)(2,1)} async-done(((bf16[192,2048]{1,0:T(8,128)(2,1)}), bf16[6144,2048]{1,0:T(8,128)(2,1)}) %all-gather.5.cloned.1.call-update) | async-done | bytes 25165840 | tf_op jit(solution)/shard_map/all_gather | solution.py:130
  372.3 14.4 %select_reduce_fusion.1 = (f32[6144]{0:T(1024)S(1)}, f32[6144,193]{0,1:T(8,128)}) fusion(pred[193]{0:T(512)(128)(4,1)S(1)} %broadcast_compare_fusion, bf16[6144,2048]{1,0:T(8,128)(2,1)} %all-gather.5.cloned.1.call-done, bf16[2048,193]{0,1:T(8,128)(2,1)S(1)} %copy-done.5), kind=kOutput, calls=%fused_computation.24 | convolution fusion | flops 4860555264 | bytes 30724288 | tf_op jit(solution)/shard_map/dot_general | solution.py:131
  386.7 75.4 %pmax.7 = f32[6144]{0:T(1024)S(1)} all-reduce(f32[6144]{0:T(1024)S(1)} %get-tuple-element.53), channel_id=1, replica_groups=mesh['kv'=8,'seq'=32] {'kv','seq'}, use_global_device_ids=true, to_apply=%region_12.13 | all-reduce | flops 6144 | bytes 49152 | tf_op jit(solution)/shard_map/pmax | solution.py:138
  462.1 4.9 multiply_reduce_fusion
  467.0 0.6 add_multiply_fusion
  467.6 0.0 all-reduce.6.cloned.1.call-update
  467.6 242.0 %all-reduce.6.cloned.1.call-done = (f32[6144]{0:T(1024)}, f32[6144]{0:T(1024)}, f32[6144]{0:T(1024)}) async-done(((f32[6144]{0:T(1024)}, f32[6144]{0:T(1024)}, f32[6144]{0:T(1024)}), (f32[6144]{0:T(1024)}, f32[6144]{0:T(1024)}, f32[6144]{0:T(1024)})) %all-reduce.6.cloned.1.call-update) | async-done | bytes 73744 | tf_op jit(solution)/shard_map/psum | solution.py:140
  709.6 0.7 log.4
  710.3 1.4 fusion.32
  (22 shorter events, 0.2 us)
Async XLA Ops:
  7.2 105.5 %copy-start = (bf16[256,2048]{1,0:T(8,128)(2,1)S(1)}, bf16[256,2048]{1,0:T(8,128)(2,1)}, u32[]{:S(2)}) copy-start(bf16[256,2048]{1,0:T(8,128)(2,1)} %param.18) | copy-start | bytes 3145732
  7.2 10.2 %copy-start.1 = (bf16[192,2048]{1,0:T(8,128)(2,1)S(1)}, bf16[192,2048]{1,0:T(8,128)(2,1)}, u32[]{:S(2)}) copy-start(bf16[192,2048]{1,0:T(8,128)(2,1)} %param.13) | copy-start | bytes 2359300
  7.2 10.2 %copy-start.6 = (f32[2048]{0:T(1024)S(1)}, f32[2048]{0:T(1024)}, u32[]{:S(2)}) copy-start(f32[2048]{0:T(1024)} %param.14) | copy-start | bytes 24580
  7.2 10.2 %copy-start.4 = (bf16[2048,256]{1,0:T(8,128)(2,1)S(1)}, bf16[2048,256]{1,0:T(8,128)(2,1)}, u32[]{:S(2)}) copy-start(bf16[2048,256]{1,0:T(8,128)(2,1)} %param.15) | copy-start | bytes 3145732
  7.2 84.0 %all-gather.3.cloned.1.call-start = ((), (), s32[]{:S(2)}) async-start(), calls=%async_computation | async-start | bytes 1622016 | tf_op jit(solution)/shard_map/all_gather | solution.py:87
  14.8 168.7 %all-reduce.4.cloned.1.call-start = ((), (), s32[]{:S(2)}) async-start(), calls=%async_computation.1 | async-start | bytes 3145728 | tf_op jit(solution)/shard_map/psum | solution.py:128
  112.6 72.7 %copy-start.3 = (f32[2048]{0:T(1024)S(1)}, f32[2048]{0:T(1024)}, u32[]{:S(2)}) copy-start(f32[2048]{0:T(1024)} %param.19) | copy-start | bytes 24580
  112.6 75.4 %copy-start.7 = (s32[193]{0:T(256)S(1)}, s32[193]{0:T(256)}, u32[]{:S(2)}) copy-start(s32[193]{0:T(256)} %param.23) | copy-start | bytes 2320
  112.6 259.7 %copy-start.5 = (bf16[2048,193]{0,1:T(8,128)(2,1)S(1)}, bf16[2048,193]{0,1:T(8,128)(2,1)}, u32[]{:S(2)}) copy-start(bf16[2048,193]{0,1:T(8,128)(2,1)} %param.20) | copy-start | bytes 2371588
  114.2 258.1 %all-gather.5.cloned.1.call-start = ((), (), s32[]{:S(2)}) async-start(), calls=%async_computation.2 | async-start | bytes 25952256 | tf_op jit(solution)/shard_map/all_gather | solution.py:130
  187.9 521.7 %all-reduce.6.cloned.1.call-start = ((), (), s32[]{:S(2)}) async-start(), calls=%async_computation.3 | async-start | bytes 147456 | tf_op jit(solution)/shard_map/psum | solution.py:140
  188.0 274.1 %copy-start.2 = (s32[6144]{0:T(1024)S(1)}, s32[6144]{0:T(1024)}, u32[]{:S(2)}) copy-start(s32[6144]{0:T(1024)} %param.22) | copy-start | bytes 73732
Sparse Core Ops, SparseCore 0:
  14.9 76.2 all-gather.2
  114.3 69.0 all-reduce.3
  188.0 184.2 all-gather.4
  467.7 241.7 all-reduce.5
where the time goes:
time: 719 us; the launch traced here: 718 us
  waiting for transfers between devices  568 us (79%)
  blocking collectives  75.4 us (10%)
  matrix products  31.1 us (4%)
  other arithmetic  21.7 us (3%)
  between operations  15.3 us (2%)
    psum x1, waiting for transfers between devices, local(): lax.psum((row_stats[1] * rescale, rescale * (row_stats[2] + (row_stats[0]...  242 us
    all_gather x1, waiting for transfers between devices, local(): head_shard_rows = lax.all_gather(final_in, 'seq', axis=0, tiled=True)  184 us
    pmax x1, blocking collectives, local(): top_all = lax.pmax(row_stats[0], ('kv', 'seq'))  75.4 us
    all_gather x1, waiting for transfers between devices, local(): shard_rows = lax.all_gather(packed, 'seq', axis=0, tiled=True)  73 us
    psum x1, waiting for transfers between devices, local(): lax.psum(jnp.dot(context, w_o, preferred_element_type=jnp.float32), 'kv')  69 us
    dot_general x1, matrix products, local(): jnp.dot(head_shard_rows, w_head, preferred_element_type=jnp.float32)  14.4 us
  transfers between devices with their start and end apart: 4, of which 4 were waited for; matrix products, arithmetic and copies ran while one was open for 0% of the time, Pallas kernels for 0%

commit v1 on v0

--- a/solution.py
+++ b/solution.py
@@ -127,7 +127,9 @@
     columns = flat_rank * vocab_local + jnp.arange(vocab_local, dtype=jnp.int32)
     attn_out = lax.psum(jnp.dot(context, w_o, preferred_element_type=jnp.float32), "kv")
     final_in = rms_norm(stream + RESID_SCALE * attn_out, final_gain).astype(jnp.bfloat16)
-    head_shard_rows = lax.all_gather(final_in, "seq", axis=0, tiled=True)
+    head_shard_rows = jnp.concatenate(
+        lax.all_to_all(jnp.stack([final_in] * lax.axis_size("seq")), "seq", 0, 0), axis=0
+    )
     logits = jnp.dot(head_shard_rows, w_head, preferred_element_type=jnp.float32) * LOGIT_SCALE
     masked = jnp.where(live_mask[None, :], logits, NEG_FILL)
     top_row = jnp.max(masked, axis=1)

time: 719 us -> 1170 us (1.63)
  waiting for transfers between devices: 568 us -> 974 us
  blocking collectives: 75.4 us -> 101 us
    all_to_all x0 -> x1, waiting for transfers between devices: none -> 589 us  [local(): lax.all_to_all(jnp.stack([final_in] * lax.axis_size('seq')), 'seq', 0, 0)]
    all_gather x1 -> x0, waiting for transfers between devices: 184 us -> none  [local(): head_shard_rows = lax.all_gather(final_in, 'seq', axis=0, tiled=True)]
    pmax x1, blocking collectives: 75.4 us -> 101 us  [local(): top_all = lax.pmax(row_stats[0], ('kv', 'seq'))]
where the time goes in v1:
time: 1170 us
  waiting for transfers between devices  974 us (83%)
  blocking collectives  101 us (9%)
  matrix products  31.2 us (3%)
  other arithmetic  20.6 us (2%)
  between operations  15.3 us (1%)
  local copies, waits for them, and re-layouts  14.7 us (1%)
    all_to_all x1, waiting for transfers between devices, local(): lax.all_to_all(jnp.stack([final_in] * lax.axis_size('seq')), 'seq', 0, 0)  589 us
    psum x1, waiting for transfers between devices, local(): lax.psum((row_stats[1] * rescale, rescale * (row_stats[2] + (row_stats[0]...  242 us
    pmax x1, blocking collectives, local(): top_all = lax.pmax(row_stats[0], ('kv', 'seq'))  101 us
    all_gather x1, waiting for transfers between devices, local(): shard_rows = lax.all_gather(packed, 'seq', axis=0, tiled=True)  73 us
    psum x1, waiting for transfers between devices, local(): lax.psum(jnp.dot(context, w_o, preferred_element_type=jnp.float32), 'kv')  69.3 us
  transfers between devices with their start and end apart: 4, of which 4 were waited for; matrix products, arithmetic and copies ran while one was open for 0% of the time, Pallas kernels for 0%

profile of v1, /device:TPU:1, one launch (start us, length us, event | category | flops | bytes accessed | tf_op | source)
XLA Modules:
  0.0 1167.0 jit_solution(17580678988797190828)
XLA Ops:
  7.2 0.0 copy-start
  7.2 0.0 copy-start.2
  7.2 0.0 copy-start.7
  7.2 0.0 copy-start.5
  7.2 0.0 all-gather.2.cloned.1.call-start
  7.3 0.9 copy.22
  8.2 0.1 reduce.2
  8.4 0.7 sub.45
  9.0 0.1 select_reduce_fusion.2
  9.1 1.4 fusion.16
  10.5 1.6 convolution_bitcast_fusion
  12.2 1.6 convolution_convert_fusion
  13.8 0.2 fusion.30
  14.0 0.7 copy.23
  14.8 0.0 all-gather.2.cloned.1.call-update
  14.8 0.0 all-reduce.4.cloned.1.call-start
  14.8 0.5 slice.24
  15.3 0.6 slice.25
  17.2 0.2 multiply_cosine_fusion
  17.4 0.0 copy-done.2
  17.5 0.6 fusion.33
  18.1 73.0 %all-gather.2.cloned.1.call-done = bf16[6144,128]{1,0:T(8,128)(2,1)} async-done(((bf16[192,128]{1,0:T(8,128)(2,1)}), bf16[6144,128]{1,0:T(8,128)(2,1)}) %all-gather.2.cloned.1.call-update) | async-done | bytes 1572880 | tf_op jit(solution)/shard_map/all_gather | solution.py:87
  91.2 21.6 %conditional.1 = (f32[1,4,192]{2,1,0:T(4,128)S(1)}, f32[1,4,192,64]{2,3,1,0:T(8,128)S(1)}) conditional(s32[]{:T(128)} %bitcast.9, (s32[6144]{0:T(1024)S(1)}, s32[6144]{0:T(1024)S(1)}, s32[192]{0:T(256)S(1)}, s32[192]{0:T(256)S(1)}, bf16[6144,128]{1,0:T(8,128)(2,1)}, /*index=5*/bf16[192,1,4,64]{0,3,2,1:T(8,128)(2,1)S(1)}) %tuple.16, () %tuple.17), branch_computations={%region_3.6_spmd, %region_6.7_spmd} | conditional | flops 1272839424 | bytes 66424336 | solution.py:117
  91.2 1.0 compare_and_fusion
  92.2 2.6 copy.25
  94.8 5.0 fusion
  99.8 6.3 fusion.7
  106.1 6.5 fusion.2
  112.7 0.0 copy-start.4
  112.8 1.6 fusion.37
  114.4 0.0 all-reduce.4.cloned.1.call-update
  114.4 69.3 %all-reduce.4.cloned.1.call-done = f32[192,2048]{1,0:T(8,128)} async-done(((f32[192,2048]{1,0:T(8,128)}), f32[192,2048]{1,0:T(8,128)}) %all-reduce.4.cloned.1.call-update) | async-done | bytes 1572880 | tf_op jit(solution)/shard_map/psum | solution.py:128
  183.6 1.7 multiply_reduce_fusion.1
  185.4 1.7 multiply_convert_fusion
  187.1 8.6 stack.2
  195.7 9.8 all-to-all-start
  205.5 0.0 all-reduce.6.cloned.1.call-start
  205.6 0.0 copy-done.8
  205.6 588.9 %all-to-all-done = bf16[32,192,2048]{2,1,0:T(8,128)(2,1)} async-done(((bf16[32,192,2048]{2,1,0:T(8,128)(2,1)}), bf16[32,192,2048]{2,1,0:T(8,128)(2,1)}, u32[]{:S(2)}, u32[]{:S(2)}) %all-to-all-start) | async-done | bytes 25165856 | tf_op jit(solution)/shard_map/all_to_all | solution.py:131
  794.5 0.0 copy-done.6
  794.5 14.5 %select_reduce_fusion.1 = (f32[6144]{0:T(1024)S(1)}, f32[6144,193]{0,1:T(8,128)}) fusion(pred[193]{0:T(512)(128)(4,1)S(1)} %broadcast_compare_fusion, bf16[6144,2048]{1,0:T(8,128)(2,1)} %bitcast.19, bf16[2048,193]{0,1:T(8,128)(2,1)S(1)} %copy-done.6), kind=kOutput, calls=%fused_computation.24 | convolution fusion | flops 4860555264 | bytes 30724288 | tf_op jit(solution)/shard_map/dot_general | solution.py:133
  809.0 101.5 %pmax.7 = f32[6144]{0:T(1024)S(1)} all-reduce(f32[6144]{0:T(1024)S(1)} %get-tuple-element.53), channel_id=1, replica_groups=mesh['kv'=8,'seq'=32] {'kv','seq'}, use_global_device_ids=true, to_apply=%region_12.13 | all-reduce | flops 6144 | bytes 49152 | tf_op jit(solution)/shard_map/pmax | solution.py:140
  910.5 4.9 multiply_reduce_fusion
  915.3 0.6 add_multiply_fusion
  916.0 0.0 all-reduce.6.cloned.1.call-update
  916.0 242.3 %all-reduce.6.cloned.1.call-done = (f32[6144]{0:T(1024)}, f32[6144]{0:T(1024)}, f32[6144]{0:T(1024)}) async-done(((f32[6144]{0:T(1024)}, f32[6144]{0:T(1024)}, f32[6144]{0:T(1024)}), (f32[6144]{0:T(1024)}, f32[6144]{0:T(1024)}, f32[6144]{0:T(1024)})) %all-reduce.6.cloned.1.call-update) | async-done | bytes 73744 | tf_op jit(solution)/shard_map/psum | solution.py:142
  1158.3 0.7 log.4
  1159.1 1.4 fusion.32
  (24 shorter events, 0.2 us)
Async XLA Ops:
  7.2 105.6 %copy-start = (bf16[256,2048]{1,0:T(8,128)(2,1)S(1)}, bf16[256,2048]{1,0:T(8,128)(2,1)}, u32[]{:S(2)}) copy-start(bf16[256,2048]{1,0:T(8,128)(2,1)} %param.18) | copy-start | bytes 3145732
  7.2 10.2 copy-start.2
  7.2 10.2 copy-start.7
  7.2 10.2 copy-start.5
  7.2 84.0 %all-gather.2.cloned.1.call-start = ((), (), s32[]{:S(2)}) async-start(), calls=%async_computation.1 | async-start | bytes 1622016 | tf_op jit(solution)/shard_map/all_gather | solution.py:87
  14.8 168.9 %all-reduce.4.cloned.1.call-start = ((), (), s32[]{:S(2)}) async-start(), calls=%async_computation.2 | async-start | bytes 3145728 | tf_op jit(solution)/shard_map/psum | solution.py:128
  112.7 72.6 %copy-start.4 = (f32[2048]{0:T(1024)S(1)}, f32[2048]{0:T(1024)}, u32[]{:S(2)}) copy-start(f32[2048]{0:T(1024)} %param.19) | copy-start | bytes 24580
  195.7 9.9 copy-start.8
  195.7 598.8 %copy-start.6 = (bf16[2048,193]{0,1:T(8,128)(2,1)S(1)}, bf16[2048,193]{0,1:T(8,128)(2,1)}, u32[]{:S(2)}) copy-start(bf16[2048,193]{0,1:T(8,128)(2,1)} %param.20) | copy-start | bytes 2371588
  195.7 598.8 %all-to-all-start = ((bf16[32,192,2048]{2,1,0:T(8,128)(2,1)}), bf16[32,192,2048]{2,1,0:T(8,128)(2,1)}, u32[]{:S(2)}, u32[]{:S(2)}) async-start(bf16[32,192,2048]{2,1,0:T(8,128)(2,1)} %stack.2), calls=%async_computation | async-start | bytes 50331648 | tf_op jit(solution)/shard_map/all_to_all | solution.py:131
  205.5 952.8 %all-reduce.6.cloned.1.call-start = ((), (), s32[]{:S(2)}) async-start(), calls=%async_computation.3 | async-start | bytes 147456 | tf_op jit(solution)/shard_map/psum | solution.py:142
  794.5 116.0 %copy-start.3 = (s32[6144]{0:T(1024)S(1)}, s32[6144]{0:T(1024)}, u32[]{:S(2)}) copy-start(s32[6144]{0:T(1024)} %param.22) | copy-start | bytes 73732
  794.5 365.9 %copy-start.1 = (bf16[256,2048]{1,0:T(8,128)(2,1)S(1)}, bf16[256,2048]{1,0:T(8,128)(2,1)}, u32[]{:S(2)}) copy-start(bf16[256,2048]{1,0:T(8,128)(2,1)} %param.18) | copy-start | bytes 3145732
Sparse Core Ops, SparseCore 0:
  14.9 76.2 all-gather.1
  114.5 69.0 all-reduce.3
  916.1 242.1 all-reduce.5
